TPU v7x, 512 devices: a whole 4x4x16 slice. The times are simulated.
512 devices in a mesh: outer: 32 (over z, x_hi), inner: 16 (over x_lo, y, core).
Axes of the slice: x: 4 (x_hi: 2, x_lo: 2; x = x_hi * 2 + x_lo), y: 4, z: 16, core: 2. Of those that a mesh axis runs over, the one named last changes fastest.
Arguments:
- queries: bfloat16 [16384, 128], P('inner'), may hold values from -150 to 150
- key_rows: bfloat16 [131072, 128], P(('outer', 'inner')), may hold values from -4.5 to 4.5
- value_rows: bfloat16 [131072, 128], P(('outer', 'inner')), may hold values from -6 to 6
Outputs:
- attended: bfloat16 [16384, 128], P('inner')
All inputs are finite; a program needn't handle non-finite values.
Results may differ from a plain program's by a relative error of at most 0.015.
Values may be sent and summed in bfloat16 or wider, within the bound.
No kernel may reach another device: no remote copies, remote signals or barrier semaphores. Data moves between devices by JAX's collectives and lax.ppermute only.
A program may use at most 64 MiB of HBM per device.

v0:
```python
import math

import jax
import jax.numpy as jnp
from jax import lax
from jax.sharding import PartitionSpec as P


def merged(part, axis, combine):
    gathered = jax.tree.map(lambda a: lax.all_gather(a, axis), part)

    def take(source):
        return jax.tree.map(lambda a: lax.dynamic_index_in_dim(a, source, 0, False), gathered)

    return lax.fori_loop(
        1, lax.axis_size(axis), lambda source, state: combine(state, take(source)), take(0)
    )


def combine_partial(left, right):
    left_sum, left_peak, left_total = left
    right_sum, right_peak, right_total = right
    joint_peak = jnp.maximum(left_peak, right_peak)
    left_factor = jnp.exp(left_peak - joint_peak)
    right_factor = jnp.exp(right_peak - joint_peak)
    joint_sum = left_sum * left_factor[:, None] + right_sum * right_factor[:, None]
    joint_total = left_total * left_factor + right_total * right_factor
    return (joint_sum, joint_peak, joint_total)


def on_device(queries, key_rows, value_rows):
    query_count, head_size = queries.shape
    score_scale = 1.0 / math.sqrt(head_size)

    def advance(running, tiles):
        weighted, row_peak, row_total = running
        key_tile, value_tile = tiles
        scores = (
            lax.dot_general(
                queries, key_tile, (((1,), (1,)), ((), ())), preferred_element_type=jnp.float32
            )
            * score_scale
        )
        new_peak = jnp.maximum(row_peak, jnp.max(scores, axis=1))
        rescale = jnp.exp(row_peak - new_peak)
        probs = jnp.exp(scores - new_peak[:, None])
        new_total = row_total * rescale + jnp.sum(probs, axis=1)
        new_weighted = weighted * rescale[:, None] + jnp.dot(
            probs.astype(jnp.bfloat16), value_tile, preferred_element_type=jnp.float32
        )
        return ((new_weighted, new_peak, new_total), None)

    start_state = (
        jnp.zeros((query_count, head_size), jnp.float32),
        jnp.full((query_count,), -1e30, jnp.float32),
        jnp.zeros((query_count,), jnp.float32),
    )
    key_part = lax.all_gather(key_rows, "inner", axis=0, tiled=True)
    value_part = lax.all_gather(value_rows, "inner", axis=0, tiled=True)
    row_count = key_part.shape[0]
    block_rows = math.gcd(row_count, 256)
    key_tiles = key_part.reshape(row_count // block_rows, block_rows, head_size)
    value_tiles = value_part.reshape(row_count // block_rows, block_rows, head_size)
    result, unused = lax.scan(advance, start_state, (key_tiles, value_tiles))
    weighted, row_peak, row_total = result
    joint_sum, joint_peak, joint_total = merged(
        (weighted, row_peak, row_total), "outer", combine_partial
    )
    attended = (joint_sum / joint_total[:, None]).astype(jnp.bfloat16)
    return attended


def solution(mesh):
    return jax.shard_map(
        on_device,
        mesh=mesh,
        in_specs=(P("inner", None), P(("outer", "inner"), None), P(("outer", "inner"), None)),
        out_specs=P("inner", None),
        check_vma=False,
    )
```

profile of v0, /device:TPU:1, one launch (start us, length us, event | category | flops | bytes accessed | tf_op | source)
XLA Modules:
  0.0 469.2 jit_solution(17336920860989906849)
XLA Ops:
  8.1 46.9 %all-gather.7.cloned.1.call-done = bf16[4096,128]{1,0:T(8,128)(2,1)} async-done(((bf16[256,128]{1,0:T(8,128)(2,1)}), bf16[4096,128]{1,0:T(8,128)(2,1)}) %all-gather.7.cloned.1.call-update) | async-done | bytes 1048592 | tf_op jit(solution)/shard_map/all_gather | solution.py:58
  55.0 42.1 %all-gather.9.cloned.1.call-done = bf16[4096,128]{1,0:T(8,128)(2,1)} async-done(((bf16[256,128]{1,0:T(8,128)(2,1)}), bf16[4096,128]{1,0:T(8,128)(2,1)}) %all-gather.9.cloned.1.call-update) | async-done | bytes 1048592 | tf_op jit(solution)/shard_map/all_gather | solution.py:59
  97.1 46.3 %while.35 = (s32[]{:T(128)}, f32[1024,128]{1,0:T(8,128)S(1)}, f32[1024]{0:T(1024)S(1)}, f32[1024]{0:T(1024)S(1)}, bf16[16,256,128]{2,1,0:T(8,128)(2,1)}, /*index...) while((s32[]{:T(128)}, f32[1024,128]{1,0:T(8,128)S(1)}, ...), condition=%wide.region_3.4_spmd.clone, body=%wide.region_0.3_spmd.clone.sunk | while | flops 136188928 | bytes 4653177 | solution.py:64
  144.3 63.4 %all-gather.2 = f32[32768]{0:T(1024)S(1)} all-gather(f32[1024]{0:T(1024)S(1)} %get-tuple-element.223), channel_id=4, replica_groups=mesh['outer'=32,'inner'=16] {'outer'}, dimensions={0}, use_global_device_ids=true | all-gather | bytes 135168 | tf_op jit(solution)/shard_map/all_gather | solution.py:10
  207.7 58.3 %all-gather.1 = f32[32768]{0:T(1024)S(1)} all-gather(f32[1024]{0:T(1024)S(1)} %get-tuple-element.222), channel_id=3, replica_groups=mesh['outer'=32,'inner'=16] {'outer'}, dimensions={0}, use_global_device_ids=true | all-gather | bytes 135168 | tf_op jit(solution)/shard_map/all_gather | solution.py:10
  266.1 146.1 %all-gather.11.cloned.1.call-done = f32[32768,128]{1,0:T(8,128)} async-done(((f32[1024,128]{1,0:T(8,128)}), f32[32768,128]{1,0:T(8,128)}) %all-gather.11.cloned.1.call-update) | async-done | bytes 16777232 | tf_op jit(solution)/shard_map/all_gather | solution.py:10
  413.2 48.5 %while.34 = (s32[]{:T(128)}, f32[1024,128]{1,0:T(8,128)S(1)}, f32[1024]{0:T(1024)S(1)}, f32[1024]{0:T(1024)S(1)}, f32[32,1024]{1,0:T(8,128)S(1)}, /*index=5*/f32...) while((s32[]{:T(128)}, f32[1024,128]{1,0:T(8,128)S(1)}, ...), condition=%wide.region_5.6_spmd, body=%wide.region_4.5_spmd.sunk | while | flops 399365 | bytes 1630351 | solution.py:15
  413.3 1.5 fusion.21
  414.8 1.5 fusion.21
  416.4 1.5 fusion.21
  418.0 1.5 fusion.21
  419.5 1.5 fusion.21
  421.1 1.5 fusion.21
  422.7 1.5 fusion.21
  424.2 1.5 fusion.21
  425.8 1.5 fusion.21
  427.4 1.5 fusion.21
  428.9 1.5 fusion.21
  430.5 1.5 fusion.21
  432.0 1.5 fusion.21
  433.6 1.5 fusion.21
  435.2 1.5 fusion.21
  436.7 1.5 fusion.21
  438.3 1.5 fusion.21
  (189 shorter events, 71.7 us)
Async XLA Ops:
  6.5 48.5 %all-gather.7.cloned.1.call-start = ((), (), s32[]{:S(2)}) async-start(), calls=%async_computation | async-start | bytes 1114112 | tf_op jit(solution)/shard_map/all_gather | solution.py:58
  7.3 89.8 %all-gather.9.cloned.1.call-start = ((), (), s32[]{:S(2)}) async-start(), calls=%async_computation.1 | async-start | bytes 1114112 | tf_op jit(solution)/shard_map/all_gather | solution.py:59
  8.0 404.1 %all-gather.11.cloned.1.call-start = ((), (), s32[]{:S(2)}) async-start(), calls=%async_computation.2 | async-start | bytes 17301504 | tf_op jit(solution)/shard_map/all_gather | solution.py:10
  143.4 0.8 copy-start
Sparse Core Ops, SparseCore 0:
  9.5 45.4 all-gather.6
  57.2 39.9 all-gather.8
  144.4 267.7 all-gather.10
where the time goes:
time: 472 us; the launch traced here: 469 us
  waiting for transfers between devices  236 us (50%)
  blocking collectives  122 us (26%)
  other arithmetic  50.8 us (11%)
  matrix products  42.5 us (9%)
  between operations  13.2 us (3%)
    all_gather x1, waiting for transfers between devices, merged(): gathered = jax.tree.map(lambda a: lax.all_gather(a, axis), part)  146 us
    all_gather x2, blocking collectives, merged(): gathered = jax.tree.map(lambda a: lax.all_gather(a, axis), part)  122 us
    all_gather x1, waiting for transfers between devices, on_device(): key_part = lax.all_gather(key_rows, 'inner', axis=0, tiled=True)  46.9 us
    add x31, other arithmetic, combine_partial(): left_sum * left_factor[:, None] + right_sum * right_factor[:, None]  46.5 us
    all_gather x1, waiting for transfers between devices, on_device(): value_part = lax.all_gather(value_rows, 'inner', axis=0, tiled=True)  42.1 us
    dot_general x16, matrix products, advance(): jnp.dot(probs.astype(jnp.bfloat16), value_tile, preferred_element_type=jn...  21.7 us
    dot_general x16, matrix products, advance(): lax.dot_general(queries, key_tile, (((1,), (1,)), ((), ())), preferred_el...  20.8 us
  transfers between devices with their start and end apart: 3, of which 3 were waited for; matrix products, arithmetic and copies ran while one was open for 0% of the time, Pallas kernels for 0%

commit v1 on v0

v1 whole, which is shorter than its diff:
```python
import functools
import math

import jax
import jax.numpy as jnp
from jax import lax
from jax.experimental import pallas as pl
from jax.experimental.pallas import tpu as pltpu
from jax.sharding import PartitionSpec as P


def attend_kernel(scale, q_ref, k_ref, v_ref, s_ref, m_ref, l_ref, acc, m_s, l_s):
    step = pl.program_id(1)

    @pl.when(step == 0)
    def _():
        acc[...] = jnp.zeros_like(acc)
        m_s[...] = jnp.full_like(m_s, -1e30)
        l_s[...] = jnp.zeros_like(l_s)

    scores = (
        lax.dot_general(
            q_ref[...], k_ref[...], (((1,), (1,)), ((), ())), preferred_element_type=jnp.float32
        )
        * scale
    )
    m_prev = m_s[...]
    m_new = jnp.maximum(m_prev, jnp.max(scores, axis=1, keepdims=True))
    rescale = jnp.exp(m_prev - m_new)
    probs = jnp.exp(scores - m_new)
    l_s[...] = l_s[...] * rescale + jnp.sum(probs, axis=1, keepdims=True)
    acc[...] = acc[...] * rescale + jnp.dot(
        probs.astype(jnp.bfloat16), v_ref[...], preferred_element_type=jnp.float32
    )
    m_s[...] = m_new

    @pl.when(step == pl.num_programs(1) - 1)
    def _():
        s_ref[...] = acc[...]
        m_ref[...] = m_s[...]
        l_ref[...] = l_s[...]


def local_partial(queries, kv, tq=512, tk=512):
    rows, head = queries.shape
    keys = kv.shape[0]
    scale = 1.0 / math.sqrt(head)
    grid = (rows // tq, keys // tk)
    return pl.pallas_call(
        functools.partial(attend_kernel, scale),
        grid=grid,
        in_specs=[
            pl.BlockSpec((tq, head), lambda i, j: (i, 0)),
            pl.BlockSpec((tk, head), lambda i, j: (j, 0)),
            pl.BlockSpec((tk, head), lambda i, j: (j, 1)),
        ],
        out_specs=[
            pl.BlockSpec((tq, head), lambda i, j: (i, 0)),
            pl.BlockSpec((tq, 1), lambda i, j: (i, 0)),
            pl.BlockSpec((tq, 1), lambda i, j: (i, 0)),
        ],
        out_shape=[
            jax.ShapeDtypeStruct((rows, head), jnp.float32),
            jax.ShapeDtypeStruct((rows, 1), jnp.float32),
            jax.ShapeDtypeStruct((rows, 1), jnp.float32),
        ],
        scratch_shapes=[
            pltpu.VMEM((tq, head), jnp.float32),
            pltpu.VMEM((tq, 1), jnp.float32),
            pltpu.VMEM((tq, 1), jnp.float32),
        ],
        compiler_params=pltpu.CompilerParams(dimension_semantics=("parallel", "arbitrary")),
        cost_estimate=pl.CostEstimate(
            flops=4 * rows * keys * head,
            transcendentals=rows * keys,
            bytes_accessed=rows * head * 6 + keys * head * 4 * grid[0],
        ),
    )(queries, kv, kv)


def on_device(queries, key_rows, value_rows):
    rows, head = queries.shape
    kv = lax.all_gather(jnp.concatenate([key_rows, value_rows], axis=1), "inner", axis=0, tiled=True)
    part_sum, part_peak, part_total = local_partial(queries, kv)

    ranges = lax.axis_size("outer")
    packed = jnp.concatenate([part_sum, part_peak, part_total], axis=1)
    got = lax.all_to_all(packed, "outer", 0, 0, tiled=True)
    got = got.reshape(ranges, rows // ranges, head + 2)
    peaks = got[:, :, head]
    joint_peak = jnp.max(peaks, axis=0)
    factor = jnp.exp(peaks - joint_peak[None])
    joint_sum = jnp.sum(got[:, :, :head] * factor[:, :, None], axis=0)
    joint_total = jnp.sum(got[:, :, head + 1] * factor, axis=0)
    mine = (joint_sum / joint_total[:, None]).astype(jnp.bfloat16)

    spread = jnp.broadcast_to(mine[None], (ranges,) + mine.shape).reshape(rows, head)
    return lax.all_to_all(spread, "outer", 0, 0, tiled=True)


def solution(mesh):
    return jax.shard_map(
        on_device,
        mesh=mesh,
        in_specs=(P("inner", None), P(("outer", "inner"), None), P(("outer", "inner"), None)),
        out_specs=P("inner", None),
        check_vma=False,
    )
```

time: 472 us -> 186 us (0.39)
  waiting for transfers between devices: 236 us -> 48.6 us
  other arithmetic: 50.8 us -> 3.71 us
  matrix products: 42.5 us -> 0 us
  blocking collectives: 122 us -> 94.9 us
  Pallas kernels: 0 us -> 23.4 us
    all_gather x3 -> x1, waiting for transfers between devices: 235 us -> 48.5 us  [on_device(): lax.all_gather(jnp.concatenate([key_rows, value_rows], axis=1), 'inner',...]
    all_gather x2 -> x0, blocking collectives: 122 us -> none  [merged(): gathered = jax.tree.map(lambda a: lax.all_gather(a, axis), part)]
    all_to_all x0 -> x2, blocking collectives: none -> 94.9 us  [the longest x1 67.6 us: on_device(): got = lax.all_to_all(packed, 'outer', 0, 0, tiled=True)]
    add x78 -> x0, other arithmetic: 47.1 us -> none  [the longest x31 46.5 us: combine_partial(): left_sum * left_factor[:, None] + right_sum * right_factor[:, None]]
    dot_general x32 -> x0, matrix products: 42.5 us -> none  [the longest x16 21.7 us: advance(): jnp.dot(probs.astype(jnp.bfloat16), value_tile, preferred_element_type=jn...]
    pallas_call x0 -> x1, Pallas kernels: none -> 23.4 us  [local_partial(): pl.pallas_call(functools.partial(attend_kernel, scale), grid=grid, in_spe...]
  transfers between devices with their start and end apart: 3 -> 1, of which waited for: 3 -> 1; matrix products, arithmetic and copies ran while one was open for 0% -> 0% of each run, Pallas kernels for 0% -> 0%
where the time goes in v1:
time: 186 us; the launch traced here: 185 us
  blocking collectives  94.9 us (51%)
  waiting for transfers between devices  48.6 us (26%)
  Pallas kernels  23.4 us (13%)
  between operations  13.4 us (7%)
  other arithmetic  3.71 us (2%)
    all_to_all x1, blocking collectives, on_device(): got = lax.all_to_all(packed, 'outer', 0, 0, tiled=True)  67.6 us
    all_gather x1, waiting for transfers between devices, on_device(): lax.all_gather(jnp.concatenate([key_rows, value_rows], axis=1), 'inner',...  48.5 us
    all_to_all x1, blocking collectives, on_device(): return lax.all_to_all(spread, 'outer', 0, 0, tiled=True)  27.3 us
    pallas_call x1, Pallas kernels, local_partial(): pl.pallas_call(functools.partial(attend_kernel, scale), grid=grid, in_spe...  23.4 us
  transfers between devices with their start and end apart: 1, of which 1 were waited for; matrix products, arithmetic and copies ran while one was open for 0% of the time, Pallas kernels for 0%

profile of v1, /device:TPU:1, one launch (start us, length us, event | category | flops | bytes accessed | tf_op | source)
XLA Modules:
  0.0 185.3 jit_solution(10857727341442570207)
XLA Ops:
  6.5 0.0 all-gather.2.cloned.1.call-start
  6.5 1.5 pad_maximum_fusion.1
  8.1 0.0 all-gather.2.cloned.1.call-update
  8.1 48.5 %all-gather.2.cloned.1.call-done.k_ref.v_ref = bf16[4096,256]{1,0:T(8,128)(2,1)} async-done(((bf16[256,256]{1,0:T(8,128)(2,1)}), bf16[4096,256]{1,0:T(8,128)(2,1)}) %all-gather.2.cloned.1.call-update) | async-done | bytes 2097168 | tf_op jit(solution)/shard_map/all_gather | solution.py:83
  56.7 23.4 %shard_map.37 = (f32[1024,128]{1,0:T(8,128)}, f32[1024,1]{1,0:T(8,128)}, f32[1024,1]{1,0:T(8,128)}) custom-call(bf16[1024,128]{1,0:T(8,128)(2,1)} %q_ref.1, bf16[4096,256]{1,0:T(8,128)(2,1)} %all-gather.2.cloned.1.call-done.k_ref.v_ref, bf16[4096,256]{1,0:T(8,128)(2,1)} %all-gather.2.cloned.1.call-done.k_ref.v_ref), custom_call_target="tpu_custom_call" | custom-call | flops 2147483648 | bytes 4980736 | tf_op jit(solution)/shard_map/pallas_call | solution.py:49
  80.1 1.6 pad_maximum_fusion
  81.7 67.6 %all_to_all.18 = f32[32,32,130]{2,1,0:T(8,128)S(1)} all-to-all(f32[32,32,130]{2,1,0:T(8,128)S(1)} %bitcast.14), channel_id=1, replica_groups=mesh['outer'=32,'inner'=16] {'outer'}, dimensions={0} | all-to-all | bytes 1064960 | tf_op jit(solution)/shard_map/all_to_all | solution.py:88
  149.3 0.3 fusion.4
  149.5 0.3 copy.16
  149.8 0.3 copy.15
  150.1 0.2 fusion
  150.3 0.1 divide_convert_fusion
  150.5 27.3 %all_to_all.19 = bf16[32,32,128]{2,1,0:T(8,128)(2,1)S(1)} all-to-all(bf16[32,32,128]{2,1,0:T(8,128)(2,1)S(1)} %broadcast_in_dim.2), channel_id=1, replica_groups=mesh['outer'=32,'inner'=16] {'outer'}, dimensions={0} | all-to-all | bytes 524288 | tf_op jit(solution)/shard_map/all_to_all | solution.py:98
  177.8 0.7 copy.19
  (3 shorter events, 0.1 us)
Async XLA Ops:
  6.5 50.1 %all-gather.2.cloned.1.call-start = ((), (), s32[]{:S(2)}) async-start(), calls=%async_computation.2 | async-start | bytes 2228224 | tf_op jit(solution)/shard_map/all_gather | solution.py:83
Sparse Core Ops, SparseCore 0:
  9.5 47.1 all-gather.1
